TPU v7x, 32 devices: a whole 2x2x4 slice. The times are simulated.
32 devices in a mesh: gz: 4 (over x, core), gy: 4 (over z), gx: 2 (over y).
Axes of the slice: x: 2, y: 2, z: 4, core: 2. Of those that a mesh axis runs over, the one named last changes fastest.
Arguments:
- volume: bfloat16 [32, 4, 32, 384], P('gz', 'gy', 'gx'), may hold values from -80 to 80
- cotangent: bfloat16 [32, 4, 32, 384], P('gz', 'gy', 'gx'), may hold values from -6 to 6
- w_project: bfloat16 [3, 384, 1152], P(None, 'gy', ('gz', 'gx')), may hold values from -0.3125 to 0.3125
- w_output: bfloat16 [3, 384, 384], P(None, 'gy', ('gz', 'gx')), may hold values from -0.3125 to 0.3125
Outputs:
- grad_volume: bfloat16 [32, 4, 32, 384], P('gz', 'gy', 'gx')
All inputs are finite; a program needn't handle non-finite values.
Results may differ from a plain program's by a relative error of at most 0.015.
Values may be sent and summed in bfloat16 or wider, within the bound.
No kernel may reach another device: no remote copies, remote signals or barrier semaphores. Data moves between devices by JAX's collectives and lax.ppermute only.
A program may use at most 64 MiB of HBM per device.

v0:
```python
import jax
import jax.numpy as jnp
from jax import lax
from jax.sharding import PartitionSpec as P

HEADS = 6


def head_norm(vector):
    return (vector * lax.rsqrt(jnp.mean(vector * vector, axis=-1, keepdims=True) + 1e-06)).astype(
        jnp.bfloat16
    )


def sublayer(line_rows, w_inner, w_outer):
    feat_len = line_rows.shape[-1]
    head_size = feat_len // HEADS
    stream = line_rows.astype(jnp.float32)
    normed = (stream * lax.rsqrt(jnp.mean(stream * stream, axis=-1, keepdims=True) + 1e-06)).astype(
        jnp.bfloat16
    )
    packed = jnp.dot(normed, w_inner, preferred_element_type=jnp.float32)
    head_shape = line_rows.shape[:3] + (HEADS, head_size)
    queries = head_norm(packed[..., :feat_len].reshape(head_shape))
    key_part = head_norm(packed[..., feat_len : 2 * feat_len].reshape(head_shape))
    value_part = packed[..., 2 * feat_len :].reshape(head_shape).astype(jnp.bfloat16)
    scores = jnp.einsum(
        "plqhe,pkqhe->pqhlk", queries, key_part, preferred_element_type=jnp.float32
    ) * head_size ** (-0.5)
    powers = jnp.exp(scores)
    attn_weights = (powers / jnp.sum(powers, axis=-1, keepdims=True)).astype(jnp.bfloat16)
    mixed_out = jnp.einsum(
        "pqhlk,pkqhe->plqhe", attn_weights, value_part, preferred_element_type=jnp.float32
    )
    mixed_out = mixed_out.astype(jnp.bfloat16).reshape(line_rows.shape)
    update = jnp.dot(mixed_out, w_outer, preferred_element_type=jnp.float32)
    return (stream + update).astype(jnp.bfloat16)


def along_depth(member, w_inner, w_outer):
    depth_len, row_len, rest_len, feat_len = member.shape
    flat_lines = member.reshape(1, depth_len, row_len * rest_len, feat_len)
    return sublayer(flat_lines, w_inner, w_outer).reshape(member.shape)


def along_rows(member, w_inner, w_outer):
    return sublayer(member, w_inner, w_outer)


def along_columns(member, w_inner, w_outer):
    depth_len, row_len, col_len, feat_len = member.shape
    flat_lines = member.reshape(depth_len * row_len, col_len, 1, feat_len)
    return sublayer(flat_lines, w_inner, w_outer).reshape(member.shape)


def backward_pass(local_fn, activ_lines, grad_lines):
    _, pullback = jax.vjp(local_fn, activ_lines)
    return pullback(grad_lines)[0]


def depth_out(stacked):
    return lax.all_to_all(stacked, "gz", split_axis=3, concat_axis=1, tiled=True)


def depth_in(stacked):
    return lax.all_to_all(stacked, "gz", split_axis=1, concat_axis=3, tiled=True)


def rows_out(stacked):
    return lax.all_to_all(stacked, "gy", split_axis=3, concat_axis=2, tiled=True)


def rows_in(stacked):
    return lax.all_to_all(stacked, "gy", split_axis=2, concat_axis=3, tiled=True)


def columns_out(stacked):
    return lax.all_to_all(stacked, "gx", split_axis=1, concat_axis=3, tiled=True)


def columns_in(stacked):
    return lax.all_to_all(stacked, "gx", split_axis=3, concat_axis=1, tiled=True)


def local(volume, cotangent, w_project, w_output):
    part_proj, part_outp = (
        lax.all_gather(w_project, "gy", axis=1, tiled=True),
        lax.all_gather(w_output, "gy", axis=1, tiled=True),
    )
    proj_full, outp_full = (
        lax.all_gather(part_proj, ("gz", "gx"), axis=2, tiled=True),
        lax.all_gather(part_outp, ("gz", "gx"), axis=2, tiled=True),
    )

    def depth_fn(member):
        return along_depth(member, proj_full[0], outp_full[0])

    def row_fn(member):
        return along_rows(member, proj_full[1], outp_full[1])

    def column_fn(member):
        return along_columns(member, proj_full[2], outp_full[2])

    depth_act = depth_out(volume[None])[0]
    field_one = depth_in(depth_fn(depth_act)[None])[0]
    row_act = rows_out(field_one[None])[0]
    field_two = rows_in(row_fn(row_act)[None])[0]
    paired = columns_out(jnp.stack([cotangent, field_two]))
    grad_two = columns_in(backward_pass(column_fn, paired[1], paired[0])[None])[0]
    row_grad = rows_out(grad_two[None])[0]
    grad_one = rows_in(backward_pass(row_fn, row_act, row_grad)[None])[0]
    depth_grad = depth_out(grad_one[None])[0]
    grad_zero = depth_in(backward_pass(depth_fn, depth_act, depth_grad)[None])[0]
    return grad_zero


def solution(mesh):
    return jax.shard_map(
        local,
        mesh=mesh,
        in_specs=(
            P("gz", "gy", "gx", None),
            P("gz", "gy", "gx", None),
            P(None, "gy", ("gz", "gx")),
            P(None, "gy", ("gz", "gx")),
        ),
        out_specs=P("gz", "gy", "gx", None),
        check_vma=False,
    )
```

profile of v0, /device:TPU:0, one launch (start us, length us, event | category | flops | bytes accessed | tf_op | source)
XLA Modules:
  0.0 244.8 jit_solution(7430313849005049411)
XLA Ops:
  7.6 21.3 %all_gather.12 = bf16[3,384,144]{2,0,1:T(4,128)(2,1)S(1)} all-gather(bf16[3,96,144]{2,0,1:T(4,128)(2,1)S(1)} %copy.364), channel_id=1, replica_groups=mesh['gz'=4,'gy'=4,'gx'=2] {'gy'}, dimensions={1}, use_global_device_ids=true | all-gather | bytes 414720 | tf_op jit(solution)/shard_map/all_gather | solution.py:87
  31.0 3.3 %all-to-all-start = ((bf16[1,8,1,16,384]{4,1,2,0,3:T(8,128)(2,1)}), bf16[1,8,1,16,384]{4,1,2,0,3:T(8,128)(2,1)S(1)}, u32[]{:S(2)}, u32[]{:S(2)}) async-start(bf16[1,8,1,16,384]{4,1,2,0,3:T(8,128)(2,1)} %bitcast.315), calls=%async_computation | async-start | bytes 196608 | tf_op jit(solution)/shard_map/all_to_all | solution.py:62
  34.4 15.0 %all_gather.14 = bf16[3,384,48]{2,0,1:T(4,128)(2,1)S(1)} all-gather(bf16[3,96,48]{2,0,1:T(4,128)(2,1)S(1)} %copy.376), channel_id=1, replica_groups=mesh['gz'=4,'gy'=4,'gx'=2] {'gy'}, dimensions={1}, use_global_device_ids=true | all-gather | bytes 138240 | tf_op jit(solution)/shard_map/all_gather | solution.py:88
  49.7 20.0 %all_gather.15 = bf16[3,384,384]{1,2,0:T(8,128)(2,1)S(1)} all-gather(bf16[3,384,48]{1,2,0:T(8,128)(2,1)S(1)} %copy.377), channel_id=1, replica_groups=mesh['gz'=4,'gy'=4,'gx'=2] {'gz','gx'}, dimensions={2}, use_global_device_ids=true | all-gather | bytes 995328 | tf_op jit(solution)/shard_map/all_gather | solution.py:92
  76.5 7.0 %all_to_all.132 = bf16[1,32,1,4,384]{4,3,2,0,1:T(4,128)(2,1)S(1)} all-to-all(bf16[1,32,1,4,384]{4,3,2,0,1:T(4,128)(2,1)S(1)} %copy.379), channel_id=1, replica_groups=mesh['gz'=4,'gy'=4,'gx'=2] {'gz'}, dimensions={1} | all-to-all | bytes 196608 | tf_op jit(solution)/shard_map/all_to_all | solution.py:66
  83.6 8.7 %all_to_all.133 = bf16[1,8,1,16,384]{4,1,2,0,3:T(8,128)(2,1)S(1)} all-to-all(bf16[1,8,1,16,384]{4,1,2,0,3:T(8,128)(2,1)S(1)} %bitcast.338), channel_id=1, replica_groups=mesh['gz'=4,'gy'=4,'gx'=2] {'gy'}, dimensions={3} | all-to-all | bytes 196608 | tf_op jit(solution)/shard_map/all_to_all | solution.py:70
  102.1 8.2 %all_to_all.134 = bf16[1,8,4,4,384]{4,1,3,0,2:T(8,128)(2,1)S(1)} all-to-all(bf16[1,8,4,4,384]{4,1,3,0,2:T(8,128)(2,1)S(1)} %fusion.28), channel_id=1, replica_groups=mesh['gz'=4,'gy'=4,'gx'=2] {'gy'}, dimensions={2} | all-to-all | bytes 196608 | tf_op jit(solution)/shard_map/all_to_all | solution.py:74
  111.2 7.2 %all_to_all.135 = bf16[2,8,1,16,384]{4,3,2,0,1:T(8,128)(2,1)S(1)} all-to-all(bf16[2,8,1,16,384]{4,3,2,0,1:T(8,128)(2,1)S(1)} %pad_maximum_fusion), channel_id=1, replica_groups=mesh['gz'=4,'gy'=4,'gx'=2] {'gx'}, dimensions={1} | all-to-all | bytes 393216 | tf_op jit(solution)/shard_map/all_to_all | solution.py:78
  126.6 1.9 reshape.731
  128.5 1.8 reshape.734
  130.3 1.9 multiply_reduce_fusion
  135.8 1.8 reshape.733
  137.6 1.7 convolution_convert_fusion.17
  139.4 1.8 reshape.729
  141.1 1.8 convert_element_type.402
  145.8 1.9 fusion.21
  153.0 1.8 reshape.735
  158.7 1.8 reshape.736
  162.9 1.9 multiply_reduce_fusion.14
  166.0 6.7 %all_to_all.136 = bf16[1,4,1,32,384]{4,1,2,0,3:T(4,128)(2,1)S(1)} all-to-all(bf16[1,4,1,32,384]{4,1,2,0,3:T(4,128)(2,1)S(1)} %copy.424), channel_id=1, replica_groups=mesh['gz'=4,'gy'=4,'gx'=2] {'gx'}, dimensions={3} | all-to-all | bytes 196608 | tf_op jit(solution)/shard_map/all_to_all | solution.py:82
  174.9 3.9 %all-to-all-start.6 = ((bf16[1,8,1,16,384]{4,1,2,0,3:T(8,128)(2,1)}), bf16[1,8,1,16,384]{4,1,2,0,3:T(8,128)(2,1)}, u32[]{:S(2)}, u32[]{:S(2)}) async-start(bf16[1,8,1,16,384]{4,1,2,0,3:T(8,128)(2,1)} %all_to_all.112), calls=%async_computation.6 | async-start | bytes 196608 | tf_op jit(solution)/shard_map/all_to_all | solution.py:70
  179.5 5.2 %all-to-all-done.6 = bf16[1,8,1,16,384]{4,1,2,0,3:T(8,128)(2,1)} async-done(((bf16[1,8,1,16,384]{4,1,2,0,3:T(8,128)(2,1)}), bf16[1,8,1,16,384]{4,1,2,0,3:T(8,128)(2,1)}, u32[]{:S(2)}, u32[]{:S(2)}) %all-to-all-start.6) | async-done | bytes 98336 | tf_op jit(solution)/shard_map/all_to_all | solution.py:70
  184.7 1.7 convolution_convert_fusion.15
  186.4 1.8 reshape.740
  188.2 2.1 fusion.14
  199.2 2.0 add_add_fusion.2
  204.6 1.7 multiply_reduce_fusion.13
  208.0 3.9 %all-to-all-start.7 = ((bf16[1,8,4,4,384]{4,1,3,0,2:T(8,128)(2,1)}), bf16[1,8,4,4,384]{4,1,3,0,2:T(8,128)(2,1)}, u32[]{:S(2)}, u32[]{:S(2)}) async-start(bf16[1,8,4,4,384]{4,1,3,0,2:T(8,128)(2,1)} %fusion.88), calls=%async_computation.7 | async-start | bytes 196608 | tf_op jit(solution)/shard_map/all_to_all | solution.py:74
  212.1 5.8 %all-to-all-done.7 = bf16[1,8,4,4,384]{4,1,3,0,2:T(8,128)(2,1)} async-done(((bf16[1,8,4,4,384]{4,1,3,0,2:T(8,128)(2,1)}), bf16[1,8,4,4,384]{4,1,3,0,2:T(8,128)(2,1)}, u32[]{:S(2)}, u32[]{:S(2)}) %all-to-all-start.7) | async-done | bytes 98336 | tf_op jit(solution)/shard_map/all_to_all | solution.py:74
  217.9 3.5 %all-to-all-start.8 = ((bf16[1,8,1,16,384]{4,1,2,0,3:T(8,128)(2,1)}), bf16[1,8,1,16,384]{4,1,2,0,3:T(8,128)(2,1)S(1)}, u32[]{:S(2)}, u32[]{:S(2)}) async-start(bf16[1,8,1,16,384]{4,1,2,0,3:T(8,128)(2,1)} %bitcast.68), calls=%async_computation.8 | async-start | bytes 196608 | tf_op jit(solution)/shard_map/all_to_all | solution.py:62
  221.5 4.0 %all-to-all-done.8 = bf16[1,8,1,16,384]{4,1,2,0,3:T(8,128)(2,1)S(1)} async-done(((bf16[1,8,1,16,384]{4,1,2,0,3:T(8,128)(2,1)}), bf16[1,8,1,16,384]{4,1,2,0,3:T(8,128)(2,1)S(1)}, u32[]{:S(2)}, u32[]{:S(2)}) %all-to-all-start.8) | async-done | bytes 98336 | tf_op jit(solution)/shard_map/all_to_all | solution.py:62
  230.6 6.7 %all_to_all.137 = bf16[1,32,1,4,384]{4,3,2,0,1:T(4,128)(2,1)S(1)} all-to-all(bf16[1,32,1,4,384]{4,3,2,0,1:T(4,128)(2,1)S(1)} %copy.469), channel_id=1, replica_groups=mesh['gz'=4,'gy'=4,'gx'=2] {'gz'}, dimensions={1} | all-to-all | bytes 196608 | tf_op jit(solution)/shard_map/all_to_all | solution.py:66
  (245 shorter events, 70.4 us)
Async XLA Ops:
  6.5 23.8 %copy-start.38 = (bf16[8,1,16,384]{3,2,1,0:T(8,128)(2,1)S(1)}, bf16[8,1,16,384]{3,2,1,0:T(8,128)(2,1)}, u32[]{:S(2)}) copy-start(bf16[8,1,16,384]{3,2,1,0:T(8,128)(2,1)} %param.4) | copy-start | bytes 294916
  6.5 27.8 %copy-start.42 = (bf16[3,96,48]{1,2,0:T(8,128)(2,1)S(1)}, bf16[3,96,48]{1,2,0:T(8,128)(2,1)}, u32[]{:S(2)}) copy-start(bf16[3,96,48]{1,2,0:T(8,128)(2,1)} %param.7) | copy-start | bytes 82948
  6.5 63.9 %all-gather.2.cloned.1.call-start = ((), (), s32[]{:S(2)}) async-start(), calls=%async_computation.10 | async-start | bytes 2985984 | tf_op jit(solution)/shard_map/all_gather | solution.py:91
  31.0 38.7 %all-to-all-start = ((bf16[1,8,1,16,384]{4,1,2,0,3:T(8,128)(2,1)}), bf16[1,8,1,16,384]{4,1,2,0,3:T(8,128)(2,1)S(1)}, u32[]{:S(2)}, u32[]{:S(2)}) async-start(bf16[1,8,1,16,384]{4,1,2,0,3:T(8,128)(2,1)} %bitcast.315), calls=%async_computation | async-start | bytes 196608 | tf_op jit(solution)/shard_map/all_to_all | solution.py:62
  69.7 6.5 %copy-start.1 = (bf16[1,8,1,16,384]{4,1,2,0,3:T(8,128)(2,1)}, bf16[1,8,1,16,384]{4,1,2,0,3:T(8,128)(2,1)S(1)}, u32[]{:S(2)}) copy-start(bf16[1,8,1,16,384]{4,1,2,0,3:T(8,128)(2,1)S(1)} %all-to-all-done) | copy-start | bytes 294916
  72.8 3.1 %copy-start.11 = (bf16[32,4,6,64]{3,2,0,1:T(8,128)(2,1)}, bf16[32,4,6,64]{3,2,0,1:T(8,128)(2,1)S(1)}, u32[]{:S(2)}) copy-start(bf16[32,4,6,64]{3,2,0,1:T(8,128)(2,1)S(1)} %convert_element_type.371) | copy-start | bytes 294916
  74.9 19.8 %copy-start.40 = (f32[4,6,32]{2,1,0:T(8,128)}, f32[4,6,32]{2,1,0:T(8,128)S(1)}, u32[]{:S(2)}) copy-start(f32[4,6,32]{2,1,0:T(8,128)S(1)} %get-tuple-element.25) | copy-start | bytes 9220
  92.3 9.5 %copy-start.3 = (bf16[1,8,1,16,384]{4,1,2,0,3:T(8,128)(2,1)}, bf16[1,8,1,16,384]{4,1,2,0,3:T(8,128)(2,1)S(1)}, u32[]{:S(2)}) copy-start(bf16[1,8,1,16,384]{4,1,2,0,3:T(8,128)(2,1)S(1)} %all_to_all.133) | copy-start | bytes 294916
  95.0 5.9 %copy-start.26 = (bf16[8,4,4,6,64]{4,3,0,2,1:T(8,128)(2,1)}, bf16[8,4,4,6,64]{4,3,0,2,1:T(8,128)(2,1)S(1)}, u32[]{:S(2)}) copy-start(bf16[8,4,4,6,64]{4,3,0,2,1:T(8,128)(2,1)S(1)} %convert_element_type.384) | copy-start | bytes 294916
  98.3 3.0 %copy-start.28 = (bf16[8,4,4,6,64]{4,0,3,2,1:T(8,128)(2,1)}, bf16[8,4,4,6,64]{4,0,3,2,1:T(8,128)(2,1)S(1)}, u32[]{:S(2)}) copy-start(bf16[8,4,4,6,64]{4,0,3,2,1:T(8,128)(2,1)S(1)} %multiply_convert_fusion.5) | copy-start | bytes 294916
  142.9 4.7 %copy-start.13 = (bf16[4,32,1,6,64]{4,3,1,0,2:T(8,128)(2,1)S(1)}, bf16[4,32,1,6,64]{4,3,1,0,2:T(8,128)(2,1)}, u32[]{:S(2)}) copy-start(bf16[4,32,1,6,64]{4,3,1,0,2:T(8,128)(2,1)} %reshape.729) | copy-start | bytes 294916
  142.9 4.7 %copy-start.14 = (bf16[4,32,6,64]{3,2,1,0:T(8,128)(2,1)S(1)}, bf16[4,32,6,64]{3,2,1,0:T(8,128)(2,1)}, u32[]{:S(2)}) copy-start(bf16[4,32,6,64]{3,2,1,0:T(8,128)(2,1)} %convert_element_type.402) | copy-start | bytes 294916
  145.8 3.8 %copy-start = (f32[4,32,1,6,64]{4,3,1,0,2:T(8,128)S(1)}, f32[4,32,1,6,64]{4,3,1,0,2:T(8,128)}, u32[]{:S(2)}) copy-start(f32[4,32,1,6,64]{4,3,1,0,2:T(8,128)} %reshape.734) | copy-start | bytes 589828
  147.9 6.9 %copy-start.37 = (f32[4,32,6]{1,0,2:T(4,128)S(1)}, f32[4,32,6]{1,0,2:T(4,128)}, u32[]{:S(2)}) copy-start(f32[4,32,6]{1,0,2:T(4,128)} %copy.401) | copy-start | bytes 9220
  156.2 4.3 %copy-start.39 = (f32[4,32,6]{1,2,0:T(8,128)S(1)}, f32[4,32,6]{1,2,0:T(8,128)}, u32[]{:S(2)}) copy-start(f32[4,32,6]{1,2,0:T(8,128)} %copy.418) | copy-start | bytes 9220
  162.9 15.9 %copy-start.10 = (f32[8,4,6,4]{3,2,1,0:T(8,128)S(1)}, f32[8,4,6,4]{3,2,1,0:T(8,128)}, u32[]{:S(2)}) copy-start(f32[8,4,6,4]{3,2,1,0:T(8,128)} %copy-done.9) | copy-start | bytes 9220
  162.9 27.4 %copy-start.6 = (f32[8,4,6,4,4]{3,4,2,1,0:T(4,128)S(1)}, f32[8,4,6,4,4]{3,4,2,1,0:T(4,128)}, u32[]{:S(2)}) copy-start(f32[8,4,6,4,4]{3,4,2,1,0:T(4,128)} %copy-done.5) | copy-start | bytes 36868
  174.9 9.8 %all-to-all-start.6 = ((bf16[1,8,1,16,384]{4,1,2,0,3:T(8,128)(2,1)}), bf16[1,8,1,16,384]{4,1,2,0,3:T(8,128)(2,1)}, u32[]{:S(2)}, u32[]{:S(2)}) async-start(bf16[1,8,1,16,384]{4,1,2,0,3:T(8,128)(2,1)} %all_to_all.112), calls=%async_computation.6 | async-start | bytes 196608 | tf_op jit(solution)/shard_map/all_to_all | solution.py:70
  188.2 3.9 %copy-start.27 = (bf16[8,4,4,6,64]{4,0,3,2,1:T(8,128)(2,1)S(1)}, bf16[8,4,4,6,64]{4,0,3,2,1:T(8,128)(2,1)}, u32[]{:S(2)}) copy-start(bf16[8,4,4,6,64]{4,0,3,2,1:T(8,128)(2,1)} %multiply_convert_fusion.4) | copy-start | bytes 294916
  188.2 5.1 %copy-start.29 = (bf16[8,4,4,6,64]{4,0,3,2,1:T(8,128)(2,1)S(1)}, bf16[8,4,4,6,64]{4,0,3,2,1:T(8,128)(2,1)}, u32[]{:S(2)}) copy-start(bf16[8,4,4,6,64]{4,0,3,2,1:T(8,128)(2,1)} %copy-done.28) | copy-start | bytes 294916
  192.2 6.8 %copy-start.23 = (f32[8,4,4,6]{3,0,2,1:T(8,128)S(1)}, f32[8,4,4,6]{3,0,2,1:T(8,128)}, u32[]{:S(2)}) copy-start(f32[8,4,4,6]{3,0,2,1:T(8,128)} %copy-done.22) | copy-start | bytes 9220
  192.2 7.0 %copy-start.21 = (f32[8,4,4,6]{0,3,2,1:T(8,128)S(1)}, f32[8,4,4,6]{0,3,2,1:T(8,128)}, u32[]{:S(2)}) copy-start(f32[8,4,4,6]{0,3,2,1:T(8,128)} %copy-done.20) | copy-start | bytes 9220
  199.2 5.4 %copy-start.4 = (bf16[1,8,1,16,384]{4,1,2,0,3:T(8,128)(2,1)S(1)}, bf16[1,8,1,16,384]{4,1,2,0,3:T(8,128)(2,1)}, u32[]{:S(2)}) copy-start(bf16[1,8,1,16,384]{4,1,2,0,3:T(8,128)(2,1)} %copy-done.3) | copy-start | bytes 294916
  202.4 3.9 %copy-start.44 = (f32[8,16]{0,1:T(8,128)S(1)}, f32[8,16]{0,1:T(8,128)}, u32[]{:S(2)}) copy-start(f32[8,16]{0,1:T(8,128)} %get-tuple-element.17) | copy-start | bytes 1540
  203.5 8.5 %copy-start.43 = (f32[4,8,4]{1,0,2:T(4,128)S(1)}, f32[4,8,4]{1,0,2:T(4,128)}, u32[]{:S(2)}) copy-start(f32[4,8,4]{1,0,2:T(4,128)} %get-tuple-element.13) | copy-start | bytes 1540
  203.5 17.9 %copy-start.41 = (f32[4,6,32]{2,1,0:T(8,128)S(1)}, f32[4,6,32]{2,1,0:T(8,128)}, u32[]{:S(2)}) copy-start(f32[4,6,32]{2,1,0:T(8,128)} %copy-done.40) | copy-start | bytes 9220
  203.5 17.9 %copy-start.32 = (f32[32,4,6]{0,1,2:T(4,128)S(1)}, f32[32,4,6]{0,1,2:T(4,128)}, u32[]{:S(2)}) copy-start(f32[32,4,6]{0,1,2:T(4,128)} %copy-done.31) | copy-start | bytes 9220
  204.4 21.5 %copy-start.8 = (f32[4,6,32,32]{2,3,1,0:T(8,128)S(1)}, f32[4,6,32,32]{2,3,1,0:T(8,128)}, u32[]{:S(2)}) copy-start(f32[4,6,32,32]{2,3,1,0:T(8,128)} %copy-done.7) | copy-start | bytes 294916
  204.6 21.5 %copy-start.12 = (bf16[32,4,6,64]{3,2,0,1:T(8,128)(2,1)S(1)}, bf16[32,4,6,64]{3,2,0,1:T(8,128)(2,1)}, u32[]{:S(2)}) copy-start(bf16[32,4,6,64]{3,2,0,1:T(8,128)(2,1)} %copy-done.11) | copy-start | bytes 294916
  206.3 20.0 %copy-start.18 = (bf16[32,4,6,64]{3,2,0,1:T(8,128)(2,1)S(1)}, bf16[32,4,6,64]{3,2,0,1:T(8,128)(2,1)}, u32[]{:S(2)}) copy-start(bf16[32,4,6,64]{3,2,0,1:T(8,128)(2,1)} %copy-done.17) | copy-start | bytes 294916
  208.0 9.8 %all-to-all-start.7 = ((bf16[1,8,4,4,384]{4,1,3,0,2:T(8,128)(2,1)}), bf16[1,8,4,4,384]{4,1,3,0,2:T(8,128)(2,1)}, u32[]{:S(2)}, u32[]{:S(2)}) async-start(bf16[1,8,4,4,384]{4,1,3,0,2:T(8,128)(2,1)} %fusion.88), calls=%async_computation.7 | async-start | bytes 196608 | tf_op jit(solution)/shard_map/all_to_all | solution.py:74
  217.9 7.6 %all-to-all-start.8 = ((bf16[1,8,1,16,384]{4,1,2,0,3:T(8,128)(2,1)}), bf16[1,8,1,16,384]{4,1,2,0,3:T(8,128)(2,1)S(1)}, u32[]{:S(2)}, u32[]{:S(2)}) async-start(bf16[1,8,1,16,384]{4,1,2,0,3:T(8,128)(2,1)} %bitcast.68), calls=%async_computation.8 | async-start | bytes 196608 | tf_op jit(solution)/shard_map/all_to_all | solution.py:62
  (18 other events, 21.1 us)
Sparse Core Ops, SparseCore 0:
  30.4 30.7 all-gather.1
where the time goes:
time: 247 us; the launch traced here: 245 us
  blocking collectives  101 us (41%)
  local copies, waits for them, and re-layouts  45.4 us (18%)
  matrix products  28.5 us (12%)
  other arithmetic  25.9 us (10%)
  waiting for transfers between devices  15 us (6%)
  starting transfers between devices  14.7 us (6%)
  between operations  14.6 us (6%)
    all_gather x1, blocking collectives, local(): lax.all_gather(w_project, 'gy', axis=1, tiled=True)  21.3 us
    all_gather x1, blocking collectives, local(): lax.all_gather(part_outp, ('gz', 'gx'), axis=2, tiled=True)  20 us
    all_gather x1, blocking collectives, local(): lax.all_gather(w_output, 'gy', axis=1, tiled=True)  15 us
    all_to_all x2, blocking collectives, depth_in(): lax.all_to_all(stacked, 'gz', split_axis=1, concat_axis=3, tiled=True)  13.7 us
    dot_general x6, matrix products, sublayer(): packed = jnp.dot(normed, w_inner, preferred_element_type=jnp.float32)  9.92 us
    all_to_all x1, blocking collectives, rows_out(): lax.all_to_all(stacked, 'gy', split_axis=3, concat_axis=2, tiled=True)  8.69 us
    all_to_all x1, blocking collectives, rows_in(): lax.all_to_all(stacked, 'gy', split_axis=2, concat_axis=3, tiled=True)  8.21 us
    dot_general x9, matrix products, sublayer(): jnp.einsum('plqhe,pkqhe->pqhlk', queries, key_part, preferred_element_typ...  7.53 us
  transfers between devices with their start and end apart: 5, of which 3 were waited for; matrix products, arithmetic and copies ran while one was open for 1% of the time, Pallas kernels for 0%

commit v1 on v0

--- a/solution.py
+++ b/solution.py
@@ -4,6 +4,22 @@
 from jax.sharding import PartitionSpec as P
 
 HEADS = 6
+
+
+def collect(x, axis, dim):
+    ways, here, turn = (lax.axis_size(axis), lax.axis_index(axis), x.shape[dim])
+    dims = [n * ways if d == dim else n for d, n in enumerate(x.shape)]
+    full = lax.dynamic_update_slice_in_dim(jnp.zeros(dims, x.dtype), x, here * turn, axis=dim)
+    going_up = going_down = x
+    for far in range(1, ways // 2 + 1):
+        going_up = lax.ppermute(going_up, axis, [(d, (d + 1) % ways) for d in range(ways)])
+        full = lax.dynamic_update_slice_in_dim(full, going_up, (here - far) % ways * turn, axis=dim)
+        if 2 * far < ways:
+            going_down = lax.ppermute(going_down, axis, [(d, (d - 1) % ways) for d in range(ways)])
+            full = lax.dynamic_update_slice_in_dim(
+                full, going_down, (here + far) % ways * turn, axis=dim
+            )
+    return full
 
 
 def head_norm(vector):
@@ -89,7 +105,7 @@
     )
     proj_full, outp_full = (
         lax.all_gather(part_proj, ("gz", "gx"), axis=2, tiled=True),
-        lax.all_gather(part_outp, ("gz", "gx"), axis=2, tiled=True),
+        collect(part_outp, ("gz", "gx"), 2),
     )
 
     def depth_fn(member):

time: 247 us -> 289 us (1.17)
  local copies, waits for them, and re-layouts: 45.4 us -> 69.4 us
  waiting for transfers between devices: 15 us -> 38.9 us
  blocking collectives: 101 us -> 82.9 us
  starting transfers between devices: 14.7 us -> 26.6 us
    dynamic_update_slice x0 -> x8, local copies, waits for them, and re-layouts: none -> 24.1 us  [the longest x4 12.3 us: collect(): lax.dynamic_update_slice_in_dim(full, going_up, (here - far) % ways * tur...]
    ppermute x0 -> x7, waiting for transfers between devices: none -> 23.9 us  [the longest x4 13 us: collect(): lax.ppermute(going_up, axis, [(d, (d + 1) % ways) for d in range(ways)])]
    all_gather x1 -> x0, blocking collectives: 20 us -> none  [local(): lax.all_gather(part_outp, ('gz', 'gx'), axis=2, tiled=True)]
    ppermute x0 -> x7, starting transfers between devices: none -> 11.6 us  [the longest x4 9 us: collect(): lax.ppermute(going_up, axis, [(d, (d + 1) % ways) for d in range(ways)])]
  transfers between devices with their start and end apart: 5 -> 12, of which waited for: 3 -> 6; matrix products, arithmetic and copies ran while one was open for 1% -> 9% of each run, Pallas kernels for 0% -> 0%
where the time goes in v1:
time: 289 us; the launch traced here: 287 us
  blocking collectives  82.9 us (29%)
  local copies, waits for them, and re-layouts  69.4 us (24%)
  waiting for transfers between devices  38.9 us (13%)
  matrix products  28.5 us (10%)
  starting transfers between devices  26.6 us (9%)
  other arithmetic  25.8 us (9%)
  between operations  14.6 us (5%)
    all_gather x1, blocking collectives, local(): lax.all_gather(w_project, 'gy', axis=1, tiled=True)  21.3 us
    all_to_all x2, blocking collectives, depth_in(): lax.all_to_all(stacked, 'gz', split_axis=1, concat_axis=3, tiled=True)  16.3 us
    all_gather x1, blocking collectives, local(): lax.all_gather(w_output, 'gy', axis=1, tiled=True)  14.5 us
    ppermute x4, waiting for transfers between devices, collect(): lax.ppermute(going_up, axis, [(d, (d + 1) % ways) for d in range(ways)])  13 us
    dynamic_update_slice x4, local copies, waits for them, and re-layouts, collect(): lax.dynamic_update_slice_in_dim(full, going_up, (here - far) % ways * tur...  12.3 us
    ppermute x3, waiting for transfers between devices, collect(): lax.ppermute(going_down, axis, [(d, (d - 1) % ways) for d in range(ways)])  10.8 us
    dot_general x6, matrix products, sublayer(): packed = jnp.dot(normed, w_inner, preferred_element_type=jnp.float32)  9.92 us
    dynamic_update_slice x3, local copies, waits for them, and re-layouts, collect(): lax.dynamic_update_slice_in_dim(full, going_down, (here + far) % ways * t...  9.59 us
  transfers between devices with their start and end apart: 12, of which 6 were waited for; matrix products, arithmetic and copies ran while one was open for 9% of the time, Pallas kernels for 0%

profile of v1, /device:TPU:0, one launch (start us, length us, event | category | flops | bytes accessed | tf_op | source)
XLA Modules:
  0.0 286.8 jit_solution(10362774706944139564)
XLA Ops:
  7.6 21.3 %all_gather.9 = bf16[3,384,144]{2,0,1:T(4,128)(2,1)S(1)} all-gather(bf16[3,96,144]{2,0,1:T(4,128)(2,1)S(1)} %copy.356), channel_id=1, replica_groups=mesh['gz'=4,'gy'=4,'gx'=2] {'gy'}, dimensions={1}, use_global_device_ids=true | all-gather | bytes 414720 | tf_op jit(solution)/shard_map/all_gather | solution.py:103
  30.4 14.5 %all_gather.11 = bf16[3,384,48]{2,1,0:T(8,128)(2,1)S(1)} all-gather(bf16[3,96,48]{2,1,0:T(8,128)(2,1)S(1)} %copy.368), channel_id=1, replica_groups=mesh['gz'=4,'gy'=4,'gx'=2] {'gy'}, dimensions={1}, use_global_device_ids=true | all-gather | bytes 138240 | tf_op jit(solution)/shard_map/all_gather | solution.py:104
  47.6 13.0 %collective-permute-done = bf16[3,384,48]{2,1,0:T(8,128)(2,1)S(1)} collective-permute-done((bf16[3,384,48]{2,1,0:T(8,128)(2,1)S(1)}, bf16[3,384,48]{2,1,0:T(8,128)(2,1)S(1)}, u32[]{:S(2)}, u32[]{:S(2)}) %collective-permute-start) | collective-permute-done | bytes 110624 | tf_op jit(solution)/shard_map/ppermute | solution.py:15
  60.6 2.5 collective-permute-start.2
  63.8 3.7 %all-to-all-start = ((bf16[1,8,1,16,384]{4,1,2,0,3:T(8,128)(2,1)}), bf16[1,8,1,16,384]{4,1,2,0,3:T(8,128)(2,1)S(1)}, u32[]{:S(2)}, u32[]{:S(2)}) async-start(bf16[1,8,1,16,384]{4,1,2,0,3:T(8,128)(2,1)} %bitcast.310), calls=%async_computation | async-start | bytes 196608 | tf_op jit(solution)/shard_map/all_to_all | solution.py:78
  67.5 2.2 dynamic_update_slice.24
  73.9 9.6 %collective-permute-done.3 = bf16[3,384,48]{2,1,0:T(8,128)(2,1)S(1)} collective-permute-done((bf16[3,384,48]{2,1,0:T(8,128)(2,1)S(1)}, bf16[3,384,48]{2,1,0:T(8,128)(2,1)S(1)}, u32[]{:S(2)}, u32[]{:S(2)}) %collective-permute-start.3) | collective-permute-done | bytes 110624 | tf_op jit(solution)/shard_map/ppermute | solution.py:18
  83.5 3.6 %collective-permute-start.6 = (bf16[3,384,48]{2,1,0:T(8,128)(2,1)S(1)}, bf16[3,384,48]{2,1,0:T(8,128)(2,1)S(1)}, u32[]{:S(2)}, u32[]{:S(2)}) collective-permute-start(bf16[3,384,48]{2,1,0:T(8,128)(2,1)S(1)} %collective-permute-done.4), channel_id=1, source_target_pairs={{0,1},{1,8},{8,9},{9,16},{16,17},{17,24},{24,25},{25,0},{2,3},{3,1... | collective-permute-start | bytes 331784 | tf_op jit(solution)/shard_map/ppermute | solution.py:15
  87.7 2.9 %dynamic_update_slice.25 = bf16[3,384,384]{2,1,0:T(8,128)(2,1)S(1)} dynamic-update-slice(bf16[3,384,384]{2,1,0:T(8,128)(2,1)S(1)} %dynamic_update_slice.24, bf16[3,384,48]{2,1,0:T(8,128)(2,1)S(1)} %collective-permute-done, s32[]{:T(128)} %constant.103.clone.1, s32[]{:T(128)} %constant.103.clone.1, s32[]{:T(128)S(6)} %select_n.57) | dynamic-update-slice | bytes 221188 | tf_op jit(solution)/shard_map/dynamic_update_slice | solution.py:16
  90.6 3.2 %dynamic_update_slice.26 = bf16[3,384,384]{2,1,0:T(8,128)(2,1)S(1)} dynamic-update-slice(bf16[3,384,384]{2,1,0:T(8,128)(2,1)S(1)} %dynamic_update_slice.25, bf16[3,384,48]{2,1,0:T(8,128)(2,1)S(1)} %collective-permute-done.1, s32[]{:T(128)} %constant.103.clone.1, s32[]{:T(128)} %constant.103.clone.1, s32[]{:T(128)S(6)} %select_n.59) | dynamic-update-slice | bytes 221188 | tf_op jit(solution)/shard_map/dynamic_update_slice | solution.py:19
  93.8 3.0 %dynamic_update_slice.27 = bf16[3,384,384]{2,1,0:T(8,128)(2,1)S(1)} dynamic-update-slice(bf16[3,384,384]{2,1,0:T(8,128)(2,1)S(1)} %dynamic_update_slice.26, bf16[3,384,48]{2,1,0:T(8,128)(2,1)S(1)} %collective-permute-done.2, s32[]{:T(128)} %constant.103.clone.1, s32[]{:T(128)} %constant.103.clone.1, s32[]{:T(128)S(6)} %select_n.61) | dynamic-update-slice | bytes 221188 | tf_op jit(solution)/shard_map/dynamic_update_slice | solution.py:16
  96.8 3.2 %dynamic_update_slice.28 = bf16[3,384,384]{2,1,0:T(8,128)(2,1)S(1)} dynamic-update-slice(bf16[3,384,384]{2,1,0:T(8,128)(2,1)S(1)} %dynamic_update_slice.27, bf16[3,384,48]{2,1,0:T(8,128)(2,1)S(1)} %collective-permute-done.3, s32[]{:T(128)} %constant.103.clone.1, s32[]{:T(128)} %constant.103.clone.1, s32[]{:T(128)S(6)} %select_n.63) | dynamic-update-slice | bytes 221188 | tf_op jit(solution)/shard_map/dynamic_update_slice | solution.py:19
  100.0 3.2 %dynamic_update_slice.29 = bf16[3,384,384]{2,1,0:T(8,128)(2,1)S(1)} dynamic-update-slice(bf16[3,384,384]{2,1,0:T(8,128)(2,1)S(1)} %dynamic_update_slice.28, bf16[3,384,48]{2,1,0:T(8,128)(2,1)S(1)} %collective-permute-done.4, s32[]{:T(128)} %constant.103.clone.1, s32[]{:T(128)} %constant.103.clone.1, s32[]{:T(128)S(6)} %select_n.65) | dynamic-update-slice | bytes 221188 | tf_op jit(solution)/shard_map/dynamic_update_slice | solution.py:16
  103.2 3.2 %dynamic_update_slice.30 = bf16[3,384,384]{2,1,0:T(8,128)(2,1)S(1)} dynamic-update-slice(bf16[3,384,384]{2,1,0:T(8,128)(2,1)S(1)} %dynamic_update_slice.29, bf16[3,384,48]{2,1,0:T(8,128)(2,1)S(1)} %collective-permute-done.5, s32[]{:T(128)} %constant.103.clone.1, s32[]{:T(128)} %constant.103.clone.1, s32[]{:T(128)S(6)} %select_n.67) | dynamic-update-slice | bytes 221188 | tf_op jit(solution)/shard_map/dynamic_update_slice | solution.py:19
  106.4 3.2 %dynamic_update_slice.31 = bf16[3,384,384]{2,1,0:T(8,128)(2,1)S(1)} dynamic-update-slice(bf16[3,384,384]{2,1,0:T(8,128)(2,1)S(1)} %dynamic_update_slice.30, bf16[3,384,48]{2,1,0:T(8,128)(2,1)S(1)} %collective-permute-done.6, s32[]{:T(128)} %constant.103.clone.1, s32[]{:T(128)} %constant.103.clone.1, s32[]{:T(128)S(6)} %select_n.69) | dynamic-update-slice | bytes 221188 | tf_op jit(solution)/shard_map/dynamic_update_slice | solution.py:16
  115.8 9.7 %all_to_all.132 = bf16[1,32,1,4,384]{4,3,2,0,1:T(4,128)(2,1)S(1)} all-to-all(bf16[1,32,1,4,384]{4,3,2,0,1:T(4,128)(2,1)S(1)} %copy.369), channel_id=1, replica_groups=mesh['gz'=4,'gy'=4,'gx'=2] {'gz'}, dimensions={1} | all-to-all | bytes 196608 | tf_op jit(solution)/shard_map/all_to_all | solution.py:82
  125.5 8.2 %all_to_all.133 = bf16[1,8,1,16,384]{4,1,2,0,3:T(8,128)(2,1)S(1)} all-to-all(bf16[1,8,1,16,384]{4,1,2,0,3:T(8,128)(2,1)S(1)} %bitcast.333), channel_id=1, replica_groups=mesh['gz'=4,'gy'=4,'gx'=2] {'gy'}, dimensions={3} | all-to-all | bytes 196608 | tf_op jit(solution)/shard_map/all_to_all | solution.py:86
  143.5 8.2 %all_to_all.134 = bf16[1,8,4,4,384]{4,1,3,0,2:T(8,128)(2,1)S(1)} all-to-all(bf16[1,8,4,4,384]{4,1,3,0,2:T(8,128)(2,1)S(1)} %fusion.28), channel_id=1, replica_groups=mesh['gz'=4,'gy'=4,'gx'=2] {'gy'}, dimensions={2} | all-to-all | bytes 196608 | tf_op jit(solution)/shard_map/all_to_all | solution.py:90
  152.6 7.7 %all_to_all.135 = bf16[2,8,1,16,384]{4,3,2,0,1:T(8,128)(2,1)S(1)} all-to-all(bf16[2,8,1,16,384]{4,3,2,0,1:T(8,128)(2,1)S(1)} %pad_maximum_fusion), channel_id=1, replica_groups=mesh['gz'=4,'gy'=4,'gx'=2] {'gx'}, dimensions={1} | all-to-all | bytes 393216 | tf_op jit(solution)/shard_map/all_to_all | solution.py:94
  172.2 1.9 multiply_reduce_fusion
  187.6 1.9 fusion.21
  204.8 1.9 multiply_reduce_fusion.14
  207.9 6.7 %all_to_all.136 = bf16[1,4,1,32,384]{4,1,2,0,3:T(4,128)(2,1)S(1)} all-to-all(bf16[1,4,1,32,384]{4,1,2,0,3:T(4,128)(2,1)S(1)} %copy.412), channel_id=1, replica_groups=mesh['gz'=4,'gy'=4,'gx'=2] {'gx'}, dimensions={3} | all-to-all | bytes 196608 | tf_op jit(solution)/shard_map/all_to_all | solution.py:98
  216.7 4.2 %all-to-all-start.6 = ((bf16[1,8,1,16,384]{4,1,2,0,3:T(8,128)(2,1)}), bf16[1,8,1,16,384]{4,1,2,0,3:T(8,128)(2,1)}, u32[]{:S(2)}, u32[]{:S(2)}) async-start(bf16[1,8,1,16,384]{4,1,2,0,3:T(8,128)(2,1)} %all_to_all.112), calls=%async_computation.6 | async-start | bytes 196608 | tf_op jit(solution)/shard_map/all_to_all | solution.py:86
  221.6 5.0 %all-to-all-done.6 = bf16[1,8,1,16,384]{4,1,2,0,3:T(8,128)(2,1)} async-done(((bf16[1,8,1,16,384]{4,1,2,0,3:T(8,128)(2,1)}), bf16[1,8,1,16,384]{4,1,2,0,3:T(8,128)(2,1)}, u32[]{:S(2)}, u32[]{:S(2)}) %all-to-all-start.6) | async-done | bytes 98336 | tf_op jit(solution)/shard_map/all_to_all | solution.py:86
  230.1 2.1 fusion.14
  241.1 2.0 add_add_fusion.2
  250.0 3.9 %all-to-all-start.7 = ((bf16[1,8,4,4,384]{4,1,3,0,2:T(8,128)(2,1)}), bf16[1,8,4,4,384]{4,1,3,0,2:T(8,128)(2,1)}, u32[]{:S(2)}, u32[]{:S(2)}) async-start(bf16[1,8,4,4,384]{4,1,3,0,2:T(8,128)(2,1)} %fusion.88), calls=%async_computation.7 | async-start | bytes 196608 | tf_op jit(solution)/shard_map/all_to_all | solution.py:90
  254.0 5.8 %all-to-all-done.7 = bf16[1,8,4,4,384]{4,1,3,0,2:T(8,128)(2,1)} async-done(((bf16[1,8,4,4,384]{4,1,3,0,2:T(8,128)(2,1)}), bf16[1,8,4,4,384]{4,1,3,0,2:T(8,128)(2,1)}, u32[]{:S(2)}, u32[]{:S(2)}) %all-to-all-start.7) | async-done | bytes 98336 | tf_op jit(solution)/shard_map/all_to_all | solution.py:90
  259.8 3.3 %all-to-all-start.8 = ((bf16[1,8,1,16,384]{4,1,2,0,3:T(8,128)(2,1)}), bf16[1,8,1,16,384]{4,1,2,0,3:T(8,128)(2,1)S(1)}, u32[]{:S(2)}, u32[]{:S(2)}) async-start(bf16[1,8,1,16,384]{4,1,2,0,3:T(8,128)(2,1)} %bitcast.68), calls=%async_computation.8 | async-start | bytes 196608 | tf_op jit(solution)/shard_map/all_to_all | solution.py:78
  263.2 4.2 %all-to-all-done.8 = bf16[1,8,1,16,384]{4,1,2,0,3:T(8,128)(2,1)S(1)} async-done(((bf16[1,8,1,16,384]{4,1,2,0,3:T(8,128)(2,1)}), bf16[1,8,1,16,384]{4,1,2,0,3:T(8,128)(2,1)S(1)}, u32[]{:S(2)}, u32[]{:S(2)}) %all-to-all-start.8) | async-done | bytes 98336 | tf_op jit(solution)/shard_map/all_to_all | solution.py:78
  272.6 6.7 %all_to_all.137 = bf16[1,32,1,4,384]{4,3,2,0,1:T(4,128)(2,1)S(1)} all-to-all(bf16[1,32,1,4,384]{4,3,2,0,1:T(4,128)(2,1)S(1)} %copy.457), channel_id=1, replica_groups=mesh['gz'=4,'gy'=4,'gx'=2] {'gz'}, dimensions={1} | all-to-all | bytes 196608 | tf_op jit(solution)/shard_map/all_to_all | solution.py:82
  (266 shorter events, 96.8 us)
Async XLA Ops:
  6.5 23.8 %copy-start.42 = (bf16[3,96,48]{1,2,0:T(8,128)(2,1)S(1)}, bf16[3,96,48]{1,2,0:T(8,128)(2,1)}, u32[]{:S(2)}) copy-start(bf16[3,96,48]{1,2,0:T(8,128)(2,1)} %param.7) | copy-start | bytes 82948
  6.5 56.6 %copy-start.38 = (bf16[8,1,16,384]{3,2,1,0:T(8,128)(2,1)S(1)}, bf16[8,1,16,384]{3,2,1,0:T(8,128)(2,1)}, u32[]{:S(2)}) copy-start(bf16[8,1,16,384]{3,2,1,0:T(8,128)(2,1)} %param.4) | copy-start | bytes 294916
  6.5 103.1 %all-gather.2.cloned.1.call-start = ((), (), s32[]{:S(2)}) async-start(), calls=%async_computation.10 | async-start | bytes 2985984 | tf_op jit(solution)/shard_map/all_gather | solution.py:107
  44.9 15.7 %collective-permute-start = (bf16[3,384,48]{2,1,0:T(8,128)(2,1)S(1)}, bf16[3,384,48]{2,1,0:T(8,128)(2,1)S(1)}, u32[]{:S(2)}, u32[]{:S(2)}) collective-permute-start(bf16[3,384,48]{2,1,0:T(8,128)(2,1)S(1)} %all_gather.11), channel_id=1, source_target_pairs={{0,1},{1,8},{8,9},{9,16},{16,17},{17,24},{24,25},{25,0},{2,3},{3,1... | collective-permute-start | bytes 331784 | tf_op jit(solution)/shard_map/ppermute | solution.py:15
  46.5 24.4 %collective-permute-start.1 = (bf16[3,384,48]{2,1,0:T(8,128)(2,1)S(1)}, bf16[3,384,48]{2,1,0:T(8,128)(2,1)S(1)}, u32[]{:S(2)}, u32[]{:S(2)}) collective-permute-start(bf16[3,384,48]{2,1,0:T(8,128)(2,1)S(1)} %all_gather.11), channel_id=1, source_target_pairs={{0,25},{1,0},{8,1},{9,8},{16,9},{17,16},{24,17},{25,24},{2,27},{3,... | collective-permute-start | bytes 331784 | tf_op jit(solution)/shard_map/ppermute | solution.py:18
  60.6 11.7 %collective-permute-start.2 = (bf16[3,384,48]{2,1,0:T(8,128)(2,1)S(1)}, bf16[3,384,48]{2,1,0:T(8,128)(2,1)S(1)}, u32[]{:S(2)}, u32[]{:S(2)}) collective-permute-start(bf16[3,384,48]{2,1,0:T(8,128)(2,1)S(1)} %collective-permute-done), channel_id=1, source_target_pairs={{0,1},{1,8},{8,9},{9,16},{16,17},{17,24},{24,25},{25,0},{2,3},{3,1... | collective-permute-start | bytes 331784 | tf_op jit(solution)/shard_map/ppermute | solution.py:15
  63.8 10.0 %all-to-all-start = ((bf16[1,8,1,16,384]{4,1,2,0,3:T(8,128)(2,1)}), bf16[1,8,1,16,384]{4,1,2,0,3:T(8,128)(2,1)S(1)}, u32[]{:S(2)}, u32[]{:S(2)}) async-start(bf16[1,8,1,16,384]{4,1,2,0,3:T(8,128)(2,1)} %bitcast.310), calls=%async_computation | async-start | bytes 196608 | tf_op jit(solution)/shard_map/all_to_all | solution.py:78
  70.9 12.6 %collective-permute-start.3 = (bf16[3,384,48]{2,1,0:T(8,128)(2,1)S(1)}, bf16[3,384,48]{2,1,0:T(8,128)(2,1)S(1)}, u32[]{:S(2)}, u32[]{:S(2)}) collective-permute-start(bf16[3,384,48]{2,1,0:T(8,128)(2,1)S(1)} %collective-permute-done.1), channel_id=1, source_target_pairs={{0,25},{1,0},{8,1},{9,8},{16,9},{17,16},{24,17},{25,24},{2,27},{3,... | collective-permute-start | bytes 331784 | tf_op jit(solution)/shard_map/ppermute | solution.py:18
  72.4 11.2 %collective-permute-start.4 = (bf16[3,384,48]{2,1,0:T(8,128)(2,1)S(1)}, bf16[3,384,48]{2,1,0:T(8,128)(2,1)S(1)}, u32[]{:S(2)}, u32[]{:S(2)}) collective-permute-start(bf16[3,384,48]{2,1,0:T(8,128)(2,1)S(1)} %collective-permute-done.2), channel_id=1, source_target_pairs={{0,1},{1,8},{8,9},{9,16},{16,17},{17,24},{24,25},{25,0},{2,3},{3,1... | collective-permute-start | bytes 331784 | tf_op jit(solution)/shard_map/ppermute | solution.py:15
  73.8 41.7 %copy-start.1 = (bf16[1,8,1,16,384]{4,1,2,0,3:T(8,128)(2,1)}, bf16[1,8,1,16,384]{4,1,2,0,3:T(8,128)(2,1)S(1)}, u32[]{:S(2)}) copy-start(bf16[1,8,1,16,384]{4,1,2,0,3:T(8,128)(2,1)S(1)} %all-to-all-done) | copy-start | bytes 294916
  83.5 19.7 %collective-permute-start.5 = (bf16[3,384,48]{2,1,0:T(8,128)(2,1)S(1)}, bf16[3,384,48]{2,1,0:T(8,128)(2,1)S(1)}, u32[]{:S(2)}, u32[]{:S(2)}) collective-permute-start(bf16[3,384,48]{2,1,0:T(8,128)(2,1)S(1)} %collective-permute-done.3), channel_id=1, source_target_pairs={{0,25},{1,0},{8,1},{9,8},{16,9},{17,16},{24,17},{25,24},{2,27},{3,... | collective-permute-start | bytes 331784 | tf_op jit(solution)/shard_map/ppermute | solution.py:18
  83.5 22.9 %collective-permute-start.6 = (bf16[3,384,48]{2,1,0:T(8,128)(2,1)S(1)}, bf16[3,384,48]{2,1,0:T(8,128)(2,1)S(1)}, u32[]{:S(2)}, u32[]{:S(2)}) collective-permute-start(bf16[3,384,48]{2,1,0:T(8,128)(2,1)S(1)} %collective-permute-done.4), channel_id=1, source_target_pairs={{0,1},{1,8},{8,9},{9,16},{16,17},{17,24},{24,25},{25,0},{2,3},{3,1... | collective-permute-start | bytes 331784 | tf_op jit(solution)/shard_map/ppermute | solution.py:15
  114.1 22.0 %copy-start.40 = (f32[4,6,32]{2,1,0:T(8,128)}, f32[4,6,32]{2,1,0:T(8,128)S(1)}, u32[]{:S(2)}) copy-start(f32[4,6,32]{2,1,0:T(8,128)S(1)} %get-tuple-element.25) | copy-start | bytes 9220
  133.7 9.5 %copy-start.3 = (bf16[1,8,1,16,384]{4,1,2,0,3:T(8,128)(2,1)}, bf16[1,8,1,16,384]{4,1,2,0,3:T(8,128)(2,1)S(1)}, u32[]{:S(2)}) copy-start(bf16[1,8,1,16,384]{4,1,2,0,3:T(8,128)(2,1)S(1)} %all_to_all.133) | copy-start | bytes 294916
  136.4 5.9 %copy-start.26 = (bf16[8,4,4,6,64]{4,3,0,2,1:T(8,128)(2,1)}, bf16[8,4,4,6,64]{4,3,0,2,1:T(8,128)(2,1)S(1)}, u32[]{:S(2)}) copy-start(bf16[8,4,4,6,64]{4,3,0,2,1:T(8,128)(2,1)S(1)} %convert_element_type.384) | copy-start | bytes 294916
  184.8 4.7 %copy-start.14 = (bf16[4,32,6,64]{3,2,1,0:T(8,128)(2,1)S(1)}, bf16[4,32,6,64]{3,2,1,0:T(8,128)(2,1)}, u32[]{:S(2)}) copy-start(bf16[4,32,6,64]{3,2,1,0:T(8,128)(2,1)} %convert_element_type.402) | copy-start | bytes 294916
  189.8 6.9 %copy-start.37 = (f32[4,32,6]{1,0,2:T(4,128)S(1)}, f32[4,32,6]{1,0,2:T(4,128)}, u32[]{:S(2)}) copy-start(f32[4,32,6]{1,0,2:T(4,128)} %copy.389) | copy-start | bytes 9220
  204.8 16.1 %copy-start.10 = (f32[8,4,6,4]{3,2,1,0:T(8,128)S(1)}, f32[8,4,6,4]{3,2,1,0:T(8,128)}, u32[]{:S(2)}) copy-start(f32[8,4,6,4]{3,2,1,0:T(8,128)} %copy-done.9) | copy-start | bytes 9220
  204.8 27.4 %copy-start.6 = (f32[8,4,6,4,4]{3,4,2,1,0:T(4,128)S(1)}, f32[8,4,6,4,4]{3,4,2,1,0:T(4,128)}, u32[]{:S(2)}) copy-start(f32[8,4,6,4,4]{3,4,2,1,0:T(4,128)} %copy-done.5) | copy-start | bytes 36868
  216.7 9.8 %all-to-all-start.6 = ((bf16[1,8,1,16,384]{4,1,2,0,3:T(8,128)(2,1)}), bf16[1,8,1,16,384]{4,1,2,0,3:T(8,128)(2,1)}, u32[]{:S(2)}, u32[]{:S(2)}) async-start(bf16[1,8,1,16,384]{4,1,2,0,3:T(8,128)(2,1)} %all_to_all.112), calls=%async_computation.6 | async-start | bytes 196608 | tf_op jit(solution)/shard_map/all_to_all | solution.py:86
  230.1 5.1 %copy-start.29 = (bf16[8,4,4,6,64]{4,0,3,2,1:T(8,128)(2,1)S(1)}, bf16[8,4,4,6,64]{4,0,3,2,1:T(8,128)(2,1)}, u32[]{:S(2)}) copy-start(bf16[8,4,4,6,64]{4,0,3,2,1:T(8,128)(2,1)} %copy-done.28) | copy-start | bytes 294916
  234.1 6.8 %copy-start.23 = (f32[8,4,4,6]{3,0,2,1:T(8,128)S(1)}, f32[8,4,4,6]{3,0,2,1:T(8,128)}, u32[]{:S(2)}) copy-start(f32[8,4,4,6]{3,0,2,1:T(8,128)} %copy-done.22) | copy-start | bytes 9220
  234.1 7.0 %copy-start.21 = (f32[8,4,4,6]{0,3,2,1:T(8,128)S(1)}, f32[8,4,4,6]{0,3,2,1:T(8,128)}, u32[]{:S(2)}) copy-start(f32[8,4,4,6]{0,3,2,1:T(8,128)} %copy-done.20) | copy-start | bytes 9220
  241.1 5.4 %copy-start.4 = (bf16[1,8,1,16,384]{4,1,2,0,3:T(8,128)(2,1)S(1)}, bf16[1,8,1,16,384]{4,1,2,0,3:T(8,128)(2,1)}, u32[]{:S(2)}) copy-start(bf16[1,8,1,16,384]{4,1,2,0,3:T(8,128)(2,1)} %copy-done.3) | copy-start | bytes 294916
  245.5 8.5 %copy-start.43 = (f32[4,8,4]{1,0,2:T(4,128)S(1)}, f32[4,8,4]{1,0,2:T(4,128)}, u32[]{:S(2)}) copy-start(f32[4,8,4]{1,0,2:T(4,128)} %get-tuple-element.13) | copy-start | bytes 1540
  245.5 17.7 %copy-start.41 = (f32[4,6,32]{2,1,0:T(8,128)S(1)}, f32[4,6,32]{2,1,0:T(8,128)}, u32[]{:S(2)}) copy-start(f32[4,6,32]{2,1,0:T(8,128)} %copy-done.40) | copy-start | bytes 9220
  245.5 17.7 %copy-start.32 = (f32[32,4,6]{0,1,2:T(4,128)S(1)}, f32[32,4,6]{0,1,2:T(4,128)}, u32[]{:S(2)}) copy-start(f32[32,4,6]{0,1,2:T(4,128)} %copy-done.31) | copy-start | bytes 9220
  246.3 21.5 %copy-start.8 = (f32[4,6,32,32]{2,3,1,0:T(8,128)S(1)}, f32[4,6,32,32]{2,3,1,0:T(8,128)}, u32[]{:S(2)}) copy-start(f32[4,6,32,32]{2,3,1,0:T(8,128)} %copy-done.7) | copy-start | bytes 294916
  246.6 21.5 %copy-start.12 = (bf16[32,4,6,64]{3,2,0,1:T(8,128)(2,1)S(1)}, bf16[32,4,6,64]{3,2,0,1:T(8,128)(2,1)}, u32[]{:S(2)}) copy-start(bf16[32,4,6,64]{3,2,0,1:T(8,128)(2,1)} %copy-done.11) | copy-start | bytes 294916
  248.3 20.1 %copy-start.18 = (bf16[32,4,6,64]{3,2,0,1:T(8,128)(2,1)S(1)}, bf16[32,4,6,64]{3,2,0,1:T(8,128)(2,1)}, u32[]{:S(2)}) copy-start(bf16[32,4,6,64]{3,2,0,1:T(8,128)(2,1)} %copy-done.17) | copy-start | bytes 294916
  250.0 9.8 %all-to-all-start.7 = ((bf16[1,8,4,4,384]{4,1,3,0,2:T(8,128)(2,1)}), bf16[1,8,4,4,384]{4,1,3,0,2:T(8,128)(2,1)}, u32[]{:S(2)}, u32[]{:S(2)}) async-start(bf16[1,8,4,4,384]{4,1,3,0,2:T(8,128)(2,1)} %fusion.88), calls=%async_computation.7 | async-start | bytes 196608 | tf_op jit(solution)/shard_map/all_to_all | solution.py:90
  259.8 7.6 %all-to-all-start.8 = ((bf16[1,8,1,16,384]{4,1,2,0,3:T(8,128)(2,1)}), bf16[1,8,1,16,384]{4,1,2,0,3:T(8,128)(2,1)S(1)}, u32[]{:S(2)}, u32[]{:S(2)}) async-start(bf16[1,8,1,16,384]{4,1,2,0,3:T(8,128)(2,1)} %bitcast.68), calls=%async_computation.8 | async-start | bytes 196608 | tf_op jit(solution)/shard_map/all_to_all | solution.py:78
  (25 other events, 48.0 us)
Sparse Core Ops, SparseCore 0:
  30.4 40.1 all-gather.1
